TPU v7x, 256 devices: a whole 4x4x8 slice. The times are simulated.
256 devices in a mesh: cells: 16 (over z, core), tracer: 16 (over y, x).
Axes of the slice: x: 4, y: 4, z: 8, core: 2. Of those that a mesh axis runs over, the one named last changes fastest.
Arguments:
- adjoint: float32 [64, 65536], P('tracer', 'cells'), may hold values from -6 to 6
- blocks: float32 [2048, 128, 128], P('cells'), may hold values from -0.375 to 0.375
- row_ptr: int32 [16, 33], P('cells'), may hold values from 0 to 128, as said below
- col_idx: int32 [2048], P('cells'), may hold values from 0 to 511, as said below
- regime: int32 [512], P('cells'), may hold values from 0 to 7
- jac: float32 [8, 64, 64], replicated, as said below
Outputs:
- sensitivity: float32 [64, 65536], P('tracer', 'cells')
Inputs may be any that keep to these rules, and one draw needn't show every extreme that they name: row_ptr[d, 0] = 0 and each block row holds 1 to 4 slots; some index of cells uses all 128 slots. `col_idx`: the first slot of each block row is its diagonal block; a live slot's column lies at most 32 blocks away from its block row, counted cyclically over the 512 blocks, and that distance is reached; slots past row_ptr[d, 32] hold any valid column. `jac`: each regime's matrix has diagonal entries of order one and off-diagonal couplings of order 0.1 between every pair of species.
All inputs are finite; a program needn't handle non-finite values.
Results may differ from a plain program's by a relative error of at most 0.0001.
Values sent between devices are 32-bit elements; how exact they have to be, the bound alone decides.
No kernel may reach another device: no remote copies, remote signals or barrier semaphores. Data moves between devices by JAX's collectives and lax.ppermute only.
A program may use at most 64 MiB of HBM per device.

v0:
```python
import jax
import jax.numpy as jnp
from jax import lax
from jax.sharding import PartitionSpec as P

BLOCK = 128
STEPS = 2


def with_halo(cells, sides, width):
    for axis, dim in sides:
        count = lax.axis_size(axis)
        head = lax.slice_in_dim(cells, 0, width, axis=dim)
        tail = lax.slice_in_dim(cells, cells.shape[dim] - width, cells.shape[dim], axis=dim)
        cells = jnp.concatenate(
            [
                lax.ppermute(tail, axis, [(i, (i + 1) % count) for i in range(count)]),
                cells,
                lax.ppermute(head, axis, [((i + 1) % count, i) for i in range(count)]),
            ],
            axis=dim,
        )
    return cells


def chemistry(moved, cell_regime, jac_table):
    result = jnp.zeros((jac_table.shape[2], moved.shape[1]), jnp.float32)
    for regime_id in range(jac_table.shape[0]):
        reacted = jnp.einsum(
            "ts,tc->sc", jac_table[regime_id], moved, precision=lax.Precision.HIGHEST
        )
        result = result + jnp.where(
            cell_regime[None, :] == regime_id, reacted, jnp.zeros_like(reacted)
        )
    return result


def body(adjoint, blocks, row_ptr, col_idx, regime, jac):
    spec_dev, cells_dev = adjoint.shape
    nb_dev = cells_dev // BLOCK
    cell_devices = lax.axis_size("cells")
    cell_index = lax.axis_index("cells")
    tracer_index = lax.axis_index("tracer")
    nb_total = nb_dev * cell_devices
    pointers = row_ptr[0]
    slot_count = blocks.shape[0]
    slot_ids = jnp.arange(slot_count)
    member = (
        (slot_ids[None, :] >= pointers[:-1, None]) & (slot_ids[None, :] < pointers[1:, None])
    ).astype(jnp.float32)
    live_slot = slot_ids < pointers[-1]
    local_col = jnp.mod(col_idx - (cell_index - 1) * nb_dev, nb_total)
    local_col = jnp.where(live_slot, local_col, 0)
    cell_regime = jnp.repeat(regime, BLOCK)
    adjoint_field = adjoint
    for hour_step in range(STEPS):
        extended = with_halo(adjoint_field, (("cells", 1),), cells_dev)
        extended_blocks = extended.reshape(spec_dev, 3 * nb_dev, BLOCK)
        picked = jnp.take(extended_blocks, local_col, axis=1, mode="clip")
        picked = jnp.where(live_slot[None, :, None], picked, jnp.zeros_like(picked))
        products = jnp.einsum("sij,qsj->qsi", blocks, picked, precision=lax.Precision.HIGHEST)
        moved = jnp.einsum(
            "rs,qsi->qri", member, products, precision=lax.Precision.HIGHEST
        ).reshape(spec_dev, cells_dev)
        whole = lax.all_gather(moved, "tracer", axis=0, tiled=True)
        species_rows = lax.dynamic_slice_in_dim(jac, tracer_index * spec_dev, spec_dev, 2)
        adjoint_field = chemistry(whole, cell_regime, species_rows)
    return adjoint_field


def solution(mesh):
    return jax.shard_map(
        body,
        mesh=mesh,
        in_specs=(
            P("tracer", "cells"),
            P("cells", None, None),
            P("cells", None),
            P("cells"),
            P("cells"),
            P(),
        ),
        out_specs=P("tracer", "cells"),
        check_vma=False,
    )
```

profile of v0, /device:TPU:2, one launch (start us, length us, event | category | flops | bytes accessed | tf_op | source)
XLA Modules:
  0.0 172.9 jit_solution(1758554243512436759)
XLA Ops:
  6.5 0.0 copy-start
  6.5 0.0 copy-start.1
  6.5 0.0 all-gather.5.cloned.1.call-start
  6.5 0.0 collective-permute-start
  6.6 5.3 %collective-permute-start.1 = (f32[4,4096]{1,0:T(4,128)}, f32[4,4096]{1,0:T(4,128)S(1)}, u32[]{:S(2)}, u32[]{:S(2)}) collective-permute-start(f32[4,4096]{1,0:T(4,128)} %param.6), channel_id=1, source_target_pairs={{16,0},{32,16},{48,32},{64,48},{80,64},{96,80},{112,96},{128,112},... | collective-permute-start | bytes 196616 | tf_op jit(solution)/shard_map/ppermute | solution.py:19
  11.9 1.2 slice.45
  13.1 0.8 slice_bitcast_fusion.1
  13.9 1.3 fusion.48
  15.2 0.7 iota_compare_fusion.2
  15.9 0.0 collective-permute-done
  15.9 0.0 collective-permute-done.1
  15.9 0.9 maximum_bitcast_fusion
  16.8 0.8 gather_fusion
  17.5 15.5 %convolution_bitcast_fusion.1 = f32[4,128,128]{2,0,1:T(4,128)S(1)} fusion(f32[128,128,128]{2,1,0:T(8,128)} %param.7, f32[128,4,128]{2,1,0:T(4,128)S(1)} %gather_fusion, pred[128]{0:T(512)(128)(4,1)S(1)} %iota_compare_fusion.2), kind=kOutput, calls=%fused_computation.33 | convolution fusion | flops 100728832 | bytes 8913024 | tf_op jit(solution)/shard_map/sij,qsj->qsi/dot_general | solution.py:61
  33.0 0.2 convolution_bitcast_fusion.3
  33.3 0.7 reshape.118
  33.9 0.0 all-gather.5.cloned.1.call-update
  34.0 0.0 all-gather.7.cloned.1.call-start
  34.0 0.0 copy-done.1
  34.0 0.1 broadcast_bitcast_fusion.6
  34.1 0.1 broadcast_bitcast_fusion.4
  34.2 0.1 broadcast_bitcast_fusion.2
  34.3 0.1 broadcast_bitcast_fusion
  34.4 47.5 %all-gather.5.cloned.1.call-done = f32[16,4,4096]{2,1,0:T(4,128)} async-done(((f32[1,4,4096]{2,1,0:T(4,128)}), f32[16,4,4096]{2,1,0:T(4,128)}) %all-gather.5.cloned.1.call-update) | async-done | bytes 1048592 | tf_op jit(solution)/shard_map/all_gather | solution.py:65
  81.8 1.6 reshape.119
  83.4 0.0 copy-done
  83.4 0.7 convolution_select_fusion.15
  84.1 0.7 fusion.13
  84.8 0.7 fusion.12
  85.5 0.7 fusion.11
  86.1 0.7 fusion.10
  86.8 0.7 fusion.9
  87.5 0.7 fusion.8
  88.1 0.7 fusion.7
  88.8 0.0 collective-permute-start.2
  88.8 2.9 %collective-permute-start.3 = (f32[4,4096]{1,0:T(4,128)S(1)}, f32[4,4096]{1,0:T(4,128)S(1)}, u32[]{:S(2)}, u32[]{:S(2)}) collective-permute-start(f32[4,4096]{1,0:T(4,128)S(1)} %fusion.7), channel_id=1, source_target_pairs={{16,0},{32,16},{48,32},{64,48},{80,64},{96,80},{112,96},{128,112},... | collective-permute-start | bytes 196616 | tf_op jit(solution)/shard_map/ppermute | solution.py:19
  91.8 1.9 %collective-permute-done.2 = f32[4,4096]{1,0:T(4,128)S(1)} collective-permute-done((f32[4,4096]{1,0:T(4,128)S(1)}, f32[4,4096]{1,0:T(4,128)S(1)}, u32[]{:S(2)}, u32[]{:S(2)}) %collective-permute-start.2) | collective-permute-done | bytes 65568 | tf_op jit(solution)/shard_map/ppermute | solution.py:17
  93.7 0.0 collective-permute-done.3
  93.8 0.8 gather_fusion.1
  94.5 15.7 %convolution_bitcast_fusion = f32[4,128,128]{2,0,1:T(4,128)S(1)} fusion(f32[128,128,128]{2,1,0:T(8,128)} %param.7, f32[128,4,128]{2,1,0:T(4,128)S(1)} %gather_fusion.1, pred[128]{0:T(512)(128)(4,1)S(1)} %iota_compare_fusion.2), kind=kOutput, calls=%fused_computation.32 | convolution fusion | flops 100728832 | bytes 8913024 | tf_op jit(solution)/shard_map/sij,qsj->qsi/dot_general | solution.py:61
  110.2 0.2 convolution_bitcast_fusion.2
  110.5 0.7 reshape.120
  111.1 0.0 all-gather.7.cloned.1.call-update
  111.2 47.4 %all-gather.7.cloned.1.call-done = f32[16,4,4096]{2,1,0:T(4,128)} async-done(((f32[1,4,4096]{2,1,0:T(4,128)}), f32[16,4,4096]{2,1,0:T(4,128)}) %all-gather.7.cloned.1.call-update) | async-done | bytes 1048592 | tf_op jit(solution)/shard_map/all_gather | solution.py:65
  158.5 1.6 reshape.121
  160.1 0.7 convolution_select_fusion.7
  160.8 0.7 fusion.6
  161.4 0.7 fusion.5
  162.1 0.7 fusion.4
  162.8 0.7 fusion.3
  163.5 0.7 fusion.2
  164.1 0.7 fusion.1
  164.8 1.3 fusion
  (3 shorter events, 0.1 us)
Async XLA Ops:
  6.5 76.9 %copy-start = (f32[8,64,64]{2,1,0:T(8,128)S(1)}, f32[8,64,64]{2,1,0:T(8,128)}, u32[]{:S(2)}) copy-start(f32[8,64,64]{2,1,0:T(8,128)} %param.11) | copy-start | bytes 393220
  6.5 27.5 %copy-start.1 = (s32[32]{0:T(128)S(1)}, s32[32]{0:T(128)}, u32[]{:S(2)}) copy-start(s32[32]{0:T(128)} %param.10) | copy-start | bytes 388
  6.5 75.3 %all-gather.5.cloned.1.call-start = ((), (), s32[]{:S(2)}) async-start(), calls=%async_computation | async-start | bytes 1114112 | tf_op jit(solution)/shard_map/all_gather | solution.py:65
  6.5 9.3 %collective-permute-start = (f32[4,4096]{1,0:T(4,128)}, f32[4,4096]{1,0:T(4,128)S(1)}, u32[]{:S(2)}, u32[]{:S(2)}) collective-permute-start(f32[4,4096]{1,0:T(4,128)} %param.6), channel_id=1, source_target_pairs={{0,16},{16,32},{32,48},{48,64},{64,80},{80,96},{96,112},{112,128},... | collective-permute-start | bytes 196616 | tf_op jit(solution)/shard_map/ppermute | solution.py:17
  6.6 9.3 %collective-permute-start.1 = (f32[4,4096]{1,0:T(4,128)}, f32[4,4096]{1,0:T(4,128)S(1)}, u32[]{:S(2)}, u32[]{:S(2)}) collective-permute-start(f32[4,4096]{1,0:T(4,128)} %param.6), channel_id=1, source_target_pairs={{16,0},{32,16},{48,32},{64,48},{80,64},{96,80},{112,96},{128,112},... | collective-permute-start | bytes 196616 | tf_op jit(solution)/shard_map/ppermute | solution.py:19
  34.0 124.5 %all-gather.7.cloned.1.call-start = ((), (), s32[]{:S(2)}) async-start(), calls=%async_computation.1 | async-start | bytes 1114112 | tf_op jit(solution)/shard_map/all_gather | solution.py:65
  88.8 4.9 %collective-permute-start.2 = (f32[4,4096]{1,0:T(4,128)S(1)}, f32[4,4096]{1,0:T(4,128)S(1)}, u32[]{:S(2)}, u32[]{:S(2)}) collective-permute-start(f32[4,4096]{1,0:T(4,128)S(1)} %fusion.7), channel_id=1, source_target_pairs={{0,16},{16,32},{32,48},{48,64},{64,80},{80,96},{96,112},{112,128},... | collective-permute-start | bytes 196616 | tf_op jit(solution)/shard_map/ppermute | solution.py:17
  88.8 4.9 %collective-permute-start.3 = (f32[4,4096]{1,0:T(4,128)S(1)}, f32[4,4096]{1,0:T(4,128)S(1)}, u32[]{:S(2)}, u32[]{:S(2)}) collective-permute-start(f32[4,4096]{1,0:T(4,128)S(1)} %fusion.7), channel_id=1, source_target_pairs={{16,0},{32,16},{48,32},{64,48},{80,64},{96,80},{112,96},{128,112},... | collective-permute-start | bytes 196616 | tf_op jit(solution)/shard_map/ppermute | solution.py:19
Sparse Core Ops, SparseCore 0:
  34.1 47.7 all-gather.4
  111.3 47.1 all-gather.6
where the time goes:
time: 173 us
  waiting for transfers between devices  96.8 us (56%)
  matrix products  42.9 us (25%)
  between operations  13.6 us (8%)
  local copies, waits for them, and re-layouts  8.35 us (5%)
  starting transfers between devices  8.32 us (5%)
  other arithmetic  2.91 us (2%)
    all_gather x2, waiting for transfers between devices, body(): whole = lax.all_gather(moved, 'tracer', axis=0, tiled=True)  94.8 us
    dot_general x2, matrix products, body(): jnp.einsum('sij,qsj->qsi', blocks, picked, precision=lax.Precision.HIGHEST)  31.2 us
    dot_general x16, matrix products, chemistry(): jnp.einsum('ts,tc->sc', jac_table[regime_id], moved, precision=lax.Precis...  11.3 us
    ppermute x2, starting transfers between devices, with_halo(): lax.ppermute(head, axis, [((i + 1) % count, i) for i in range(count)])  8.25 us
    unnamed x8, local copies, waits for them, and re-layouts  4.5 us
  transfers between devices with their start and end apart: 6, of which 3 were waited for; matrix products, arithmetic and copies ran while one was open for 2% of the time, Pallas kernels for 0%

commit v1 on v0

--- a/solution.py
+++ b/solution.py
@@ -62,7 +62,9 @@
         moved = jnp.einsum(
             "rs,qsi->qri", member, products, precision=lax.Precision.HIGHEST
         ).reshape(spec_dev, cells_dev)
-        whole = lax.all_gather(moved, "tracer", axis=0, tiled=True)
+        whole = jnp.concatenate(
+            lax.all_to_all(jnp.stack([moved] * lax.axis_size("tracer")), "tracer", 0, 0), axis=0
+        )
         species_rows = lax.dynamic_slice_in_dim(jac, tracer_index * spec_dev, spec_dev, 2)
         adjoint_field = chemistry(whole, cell_regime, species_rows)
     return adjoint_field

time: 173 us -> 105 us (0.61)
  waiting for transfers between devices: 96.8 us -> 15 us
  blocking collectives: 0 us -> 20.9 us
  between operations: 13.6 us -> 0.23 us
  starting transfers between devices: 8.32 us -> 15.8 us
  local copies, waits for them, and re-layouts: 8.35 us -> 6.04 us
    all_gather x2 -> x0, waiting for transfers between devices: 94.8 us -> none  [body(): whole = lax.all_gather(moved, 'tracer', axis=0, tiled=True)]
    all_to_all x0 -> x1, blocking collectives: none -> 20.9 us  [body(): lax.all_to_all(jnp.stack([moved] * lax.axis_size('tracer')), 'tracer', 0, 0)]
    all_to_all x0 -> x1, waiting for transfers between devices: none -> 13.1 us  [body(): lax.all_to_all(jnp.stack([moved] * lax.axis_size('tracer')), 'tracer', 0, 0)]
    all_to_all x0 -> x1, starting transfers between devices: none -> 7.48 us  [body(): lax.all_to_all(jnp.stack([moved] * lax.axis_size('tracer')), 'tracer', 0, 0)]
    unnamed x8 -> x6, local copies, waits for them, and re-layouts: 4.5 us -> 0.1 us
  transfers between devices with their start and end apart: 6 -> 5, of which waited for: 3 -> 2; matrix products, arithmetic and copies ran while one was open for 2% -> 4% of each run, Pallas kernels for 0% -> 0%
where the time goes in v1:
time: 105 us; the launch traced here: 104 us
  matrix products  42.8 us (41%)
  blocking collectives  20.9 us (20%)
  starting transfers between devices  15.8 us (15%)
  waiting for transfers between devices  15 us (14%)
  local copies, waits for them, and re-layouts  6.04 us (6%)
  other arithmetic  2.91 us (3%)
    dot_general x2, matrix products, body(): jnp.einsum('sij,qsj->qsi', blocks, picked, precision=lax.Precision.HIGHEST)  31 us
    all_to_all x1, blocking collectives, body(): lax.all_to_all(jnp.stack([moved] * lax.axis_size('tracer')), 'tracer', 0, 0)  20.9 us
    all_to_all x1, waiting for transfers between devices, body(): lax.all_to_all(jnp.stack([moved] * lax.axis_size('tracer')), 'tracer', 0, 0)  13.1 us
    dot_general x16, matrix products, chemistry(): jnp.einsum('ts,tc->sc', jac_table[regime_id], moved, precision=lax.Precis...  11.3 us
    ppermute x2, starting transfers between devices, with_halo(): lax.ppermute(head, axis, [((i + 1) % count, i) for i in range(count)])  8.25 us
    all_to_all x1, starting transfers between devices, body(): lax.all_to_all(jnp.stack([moved] * lax.axis_size('tracer')), 'tracer', 0, 0)  7.48 us
  transfers between devices with their start and end apart: 5, of which 2 were waited for; matrix products, arithmetic and copies ran while one was open for 4% of the time, Pallas kernels for 0%

profile of v1, /device:TPU:2, one launch (start us, length us, event | category | flops | bytes accessed | tf_op | source)
XLA Modules:
  0.0 103.6 jit_solution(2038492601452350623)
XLA Ops:
  0.0 0.0 copy-start
  0.0 0.0 copy-start.1
  0.0 0.0 collective-permute-start
  0.0 5.3 %collective-permute-start.1 = (f32[4,4096]{1,0:T(4,128)}, f32[4,4096]{1,0:T(4,128)S(1)}, u32[]{:S(2)}, u32[]{:S(2)}) collective-permute-start(f32[4,4096]{1,0:T(4,128)} %param.6), channel_id=1, source_target_pairs={{16,0},{32,16},{48,32},{64,48},{80,64},{96,80},{112,96},{128,112},... | collective-permute-start | bytes 196616 | tf_op jit(solution)/shard_map/ppermute | solution.py:19
  5.3 1.2 %slice.45 = s32[1,1]{1,0:T(1,128)} slice(s32[1,33]{1,0:T(1,128)} %param.8), slice={[0:1], [32:33]} | slice | bytes 8 | tf_op jit(solution)/shard_map/slice | solution.py:51
  6.6 0.8 slice_bitcast_fusion.1
  7.4 1.3 %fusion.52 = s32[128]{0:T(128)S(1)} fusion(s32[128]{0:T(128)} %param.9, s32[]{:T(128)S(6)} %mul.8, s32[]{:T(128)} %bitcast.2), kind=kLoop, calls=%fused_computation.96 | loop fusion | flops 1792 | bytes 1032 | tf_op jit(solution)/shard_map/jit(_where)/select_n | solution.py:53
  8.7 0.7 iota_compare_fusion.2
  9.3 0.0 collective-permute-done
  9.3 0.0 collective-permute-done.1
  9.4 0.9 maximum_bitcast_fusion
  10.2 0.8 gather_fusion
  11.0 15.5 %fusion.18 = f32[128,4,128]{2,1,0:T(4,128)S(1)} fusion(f32[128,128,128]{2,1,0:T(8,128)} %param.7, f32[128,4,128]{2,1,0:T(4,128)S(1)} %gather_fusion, pred[128]{0:T(512)(128)(4,1)S(1)} %iota_compare_fusion.2), kind=kOutput, calls=%fused_computation.38 | convolution fusion | flops 100728832 | bytes 8913024 | tf_op jit(solution)/shard_map/sij,qsj->qsi/dot_general | solution.py:61
  26.5 0.2 convolution_bitcast_fusion.1
  26.8 1.2 %stack.6 = f32[16,4,4096]{2,1,0:T(4,128)} broadcast(f32[4,4096]{1,0:T(4,128)S(1)} %bitcast.103), dimensions={1,2} | broadcast | bytes 1114112 | tf_op jit(solution)/shard_map/stack | solution.py:66
  28.0 7.5 %all-to-all-start = ((f32[16,4,4096]{2,1,0:T(4,128)}), f32[16,4,4096]{2,1,0:T(4,128)S(1)}, u32[]{:S(2)}, u32[]{:S(2)}) async-start(f32[16,4,4096]{2,1,0:T(4,128)} %stack.6), calls=%async_computation | async-start | bytes 2097152 | tf_op jit(solution)/shard_map/all_to_all | solution.py:66
  35.5 0.0 copy-done.1
  35.5 0.1 broadcast_bitcast_fusion.6
  35.6 0.1 broadcast_bitcast_fusion.4
  35.6 0.1 broadcast_bitcast_fusion.2
  35.7 0.1 broadcast_bitcast_fusion
  35.8 13.1 %all-to-all-done = f32[16,4,4096]{2,1,0:T(4,128)S(1)} async-done(((f32[16,4,4096]{2,1,0:T(4,128)}), f32[16,4,4096]{2,1,0:T(4,128)S(1)}, u32[]{:S(2)}, u32[]{:S(2)}) %all-to-all-start) | async-done | bytes 1048608 | tf_op jit(solution)/shard_map/all_to_all | solution.py:66
  48.9 0.4 reshape.101
  49.2 0.0 copy-done
  49.2 0.7 convolution_select_fusion.15
  49.9 0.7 fusion.13
  50.6 0.7 fusion.12
  51.3 0.7 fusion.11
  51.9 0.7 fusion.10
  52.6 0.7 fusion.9
  53.3 0.7 fusion.8
  54.0 0.7 fusion.7
  54.6 0.0 collective-permute-start.2
  54.6 2.9 %collective-permute-start.3 = (f32[4,4096]{1,0:T(4,128)S(1)}, f32[4,4096]{1,0:T(4,128)S(1)}, u32[]{:S(2)}, u32[]{:S(2)}) collective-permute-start(f32[4,4096]{1,0:T(4,128)S(1)} %fusion.7), channel_id=1, source_target_pairs={{16,0},{32,16},{48,32},{64,48},{80,64},{96,80},{112,96},{128,112},... | collective-permute-start | bytes 196616 | tf_op jit(solution)/shard_map/ppermute | solution.py:19
  57.6 1.9 %collective-permute-done.2 = f32[4,4096]{1,0:T(4,128)S(1)} collective-permute-done((f32[4,4096]{1,0:T(4,128)S(1)}, f32[4,4096]{1,0:T(4,128)S(1)}, u32[]{:S(2)}, u32[]{:S(2)}) %collective-permute-start.2) | collective-permute-done | bytes 65568 | tf_op jit(solution)/shard_map/ppermute | solution.py:17
  59.5 0.0 collective-permute-done.3
  59.6 0.8 gather_fusion.1
  60.3 15.5 %fusion.15 = f32[128,4,128]{2,1,0:T(4,128)S(1)} fusion(f32[128,128,128]{2,1,0:T(8,128)} %param.7, f32[128,4,128]{2,1,0:T(4,128)S(1)} %gather_fusion.1, pred[128]{0:T(512)(128)(4,1)S(1)} %iota_compare_fusion.2), kind=kOutput, calls=%fused_computation.35 | convolution fusion | flops 100728832 | bytes 8913024 | tf_op jit(solution)/shard_map/sij,qsj->qsi/dot_general | solution.py:61
  75.8 0.2 convolution_bitcast_fusion
  76.1 0.2 stack.7
  76.3 20.9 %all_to_all.10 = f32[16,4,4096]{2,1,0:T(4,128)S(1)} all-to-all(f32[16,4,4096]{2,1,0:T(4,128)S(1)} %stack.7), channel_id=1, replica_groups=mesh['cells'=16,'tracer'=16] {'tracer'}, dimensions={0} | all-to-all | bytes 2097152 | tf_op jit(solution)/shard_map/all_to_all | solution.py:66
  97.2 0.4 reshape.103
  97.6 0.7 convolution_select_fusion.7
  98.3 0.7 fusion.6
  98.9 0.7 fusion.5
  99.6 0.7 fusion.4
  100.3 0.7 fusion.3
  100.9 0.7 fusion.2
  101.6 0.7 fusion.1
  102.3 1.3 %fusion = f32[4,4096]{1,0:T(4,128)} fusion(f32[4,4096]{1,0:T(4,128)S(1)} %fusion.1, f32[64,4096]{1,0:T(8,128)S(1)} %reshape.103, pred[4096]{0:T(1024)(128)(4,1)S(1)} %get-tuple-element.15, f32[8,64,64]{2,1,0:T(8,128)S(1)} %copy-done, s32[]{:T(128)S(6)} %add.75, s32[]{:T(128)S(6)} %select_n.71), kind=kOutput, calls=%fused_computation.3 | convolution fusion | flops 12615680 | bytes 1216520 | tf_op jit(solution)/shard_map/ts,tc->sc/dot_general | solution.py:29
  (5 shorter events, 0.2 us)
Async XLA Ops:
  0.0 49.2 %copy-start = (f32[8,64,64]{2,1,0:T(8,128)S(1)}, f32[8,64,64]{2,1,0:T(8,128)}, u32[]{:S(2)}) copy-start(f32[8,64,64]{2,1,0:T(8,128)} %param.11) | copy-start | bytes 393220
  0.0 35.5 %copy-start.1 = (s32[32]{0:T(128)S(1)}, s32[32]{0:T(128)}, u32[]{:S(2)}) copy-start(s32[32]{0:T(128)} %param.10) | copy-start | bytes 388
  0.0 9.3 %collective-permute-start = (f32[4,4096]{1,0:T(4,128)}, f32[4,4096]{1,0:T(4,128)S(1)}, u32[]{:S(2)}, u32[]{:S(2)}) collective-permute-start(f32[4,4096]{1,0:T(4,128)} %param.6), channel_id=1, source_target_pairs={{0,16},{16,32},{32,48},{48,64},{64,80},{80,96},{96,112},{112,128},... | collective-permute-start | bytes 196616 | tf_op jit(solution)/shard_map/ppermute | solution.py:17
  0.0 9.3 %collective-permute-start.1 = (f32[4,4096]{1,0:T(4,128)}, f32[4,4096]{1,0:T(4,128)S(1)}, u32[]{:S(2)}, u32[]{:S(2)}) collective-permute-start(f32[4,4096]{1,0:T(4,128)} %param.6), channel_id=1, source_target_pairs={{16,0},{32,16},{48,32},{64,48},{80,64},{96,80},{112,96},{128,112},... | collective-permute-start | bytes 196616 | tf_op jit(solution)/shard_map/ppermute | solution.py:19
  28.0 20.9 %all-to-all-start = ((f32[16,4,4096]{2,1,0:T(4,128)}), f32[16,4,4096]{2,1,0:T(4,128)S(1)}, u32[]{:S(2)}, u32[]{:S(2)}) async-start(f32[16,4,4096]{2,1,0:T(4,128)} %stack.6), calls=%async_computation | async-start | bytes 2097152 | tf_op jit(solution)/shard_map/all_to_all | solution.py:66
  54.6 4.9 %collective-permute-start.2 = (f32[4,4096]{1,0:T(4,128)S(1)}, f32[4,4096]{1,0:T(4,128)S(1)}, u32[]{:S(2)}, u32[]{:S(2)}) collective-permute-start(f32[4,4096]{1,0:T(4,128)S(1)} %fusion.7), channel_id=1, source_target_pairs={{0,16},{16,32},{32,48},{48,64},{64,80},{80,96},{96,112},{112,128},... | collective-permute-start | bytes 196616 | tf_op jit(solution)/shard_map/ppermute | solution.py:17
  54.6 4.9 %collective-permute-start.3 = (f32[4,4096]{1,0:T(4,128)S(1)}, f32[4,4096]{1,0:T(4,128)S(1)}, u32[]{:S(2)}, u32[]{:S(2)}) collective-permute-start(f32[4,4096]{1,0:T(4,128)S(1)} %fusion.7), channel_id=1, source_target_pairs={{16,0},{32,16},{48,32},{64,48},{80,64},{96,80},{112,96},{128,112},... | collective-permute-start | bytes 196616 | tf_op jit(solution)/shard_map/ppermute | solution.py:19
